TPU v7x, 256 devices: a whole 4x4x8 slice. The times are simulated.
256 devices in a mesh: ctx: 32 (over z, x), tp: 8 (over y, core).
Axes of the slice: x: 4, y: 4, z: 8, core: 2. Of those that a mesh axis runs over, the one named last changes fastest.
Arguments:
- tokens: bfloat16 [16384, 3072], P(('ctx', 'tp')), may hold values from -6 to 6
- w_query: bfloat16 [3072, 4096], P(None, 'tp'), may hold values from -0.109375 to 0.109375
- w_key: bfloat16 [3072, 4096], P(None, 'tp'), may hold values from -0.109375 to 0.109375
- w_value: bfloat16 [3072, 4096], P(None, 'tp'), may hold values from -0.109375 to 0.109375
- norm_gain: float32 [4096], P('tp'), may hold values from 0.1 to 1.9
Outputs:
- attended: bfloat16 [16384, 4096], P('ctx', 'tp')
All inputs are finite; a program needn't handle non-finite values.
Results may differ from a plain program's by a relative error of at most 0.0062.
Values may be sent and summed in bfloat16 or wider, within the bound.
No kernel may reach another device: no remote copies, remote signals or barrier semaphores. Data moves between devices by JAX's collectives and lax.ppermute only.
A program may use at most 64 MiB of HBM per device.

v0:
```python
import jax
import jax.numpy as jnp
from jax import lax
from jax.sharding import PartitionSpec as P

HEAD_DIM = 128
BLOCK = 512
EPSILON = 1e-06


def from_behind(value, axis, by):
    size = lax.axis_size(axis)
    pairs = [(i, i + by) for i in range(size) if 0 <= i + by < size]
    return lax.ppermute(value, axis, pairs)


def body(tokens, w_query, w_key, w_value, norm_gain):
    local_width = w_query.shape[1]
    head_count = local_width // HEAD_DIM
    piece_rows = lax.all_gather(tokens, "tp", axis=0, tiled=True)
    query_part = jnp.dot(piece_rows, w_query, preferred_element_type=jnp.float32).astype(
        jnp.bfloat16
    )
    key_part = jnp.dot(piece_rows, w_key, preferred_element_type=jnp.float32).astype(jnp.bfloat16)
    value_part = jnp.dot(piece_rows, w_value, preferred_element_type=jnp.float32).astype(
        jnp.bfloat16
    )
    projected = jnp.concatenate([query_part, key_part, value_part], axis=1)
    group_len = projected.shape[0]
    block_count = group_len // BLOCK
    shaped = projected.reshape(block_count, BLOCK, 3, head_count, HEAD_DIM)
    query_rows = shaped[:, :, 0]
    key_rows = shaped[:, :, 1]
    value_rows = shaped[:, :, 2]
    block_states = jnp.einsum(
        "bshd,bshe->bhde", key_rows, value_rows, preferred_element_type=jnp.float32
    )
    local_state = jnp.sum(block_states, axis=0)
    empty_state = jnp.zeros_like(local_state)

    def advance(step_index, carried):
        return from_behind(carried + local_state, "ctx", 1)

    prefix_state = lax.fori_loop(0, lax.axis_size("ctx") - 1, advance, empty_state)
    running = jnp.cumsum(block_states, axis=0)
    earlier = jnp.concatenate([jnp.zeros_like(block_states), running[:-1]], axis=0)
    block_start = prefix_state[None] + earlier
    scores = jnp.einsum("bqhd,bkhd->bhqk", query_rows, key_rows, preferred_element_type=jnp.float32)
    causal = jnp.arange(BLOCK)[:, None] >= jnp.arange(BLOCK)[None, :]
    scores = jnp.where(causal[None, None], scores, jnp.float32(0.0)).astype(jnp.bfloat16)
    inner = jnp.einsum("bhqk,bkhe->bqhe", scores, value_rows, preferred_element_type=jnp.float32)
    carried_part = jnp.einsum(
        "bqhd,bhde->bqhe",
        query_rows.astype(jnp.float32),
        block_start,
        precision=lax.Precision.HIGHEST,
    )
    mixed = inner + carried_part
    mean_square = jnp.mean(mixed * mixed, axis=-1, keepdims=True)
    normed = mixed * lax.rsqrt(mean_square + EPSILON) * norm_gain.reshape(head_count, HEAD_DIM)
    return normed.reshape(group_len, local_width).astype(jnp.bfloat16)


def solution(mesh):
    placed = (P(("ctx", "tp"), None), P(None, "tp"), P(None, "tp"), P(None, "tp"), P("tp"))
    return jax.shard_map(
        body, mesh=mesh, in_specs=placed, out_specs=P("ctx", "tp"), check_vma=False
    )
```

profile of v0, /device:TPU:128, one launch (start us, length us, event | category | flops | bytes accessed | tf_op | source)
XLA Modules:
  0.0 505.0 jit_solution(23542777974359117)
XLA Ops:
  8.0 32.9 %all-gather.2.cloned.1.call-done = bf16[512,3072]{1,0:T(8,128)(2,1)} async-done(((bf16[64,3072]{1,0:T(8,128)(2,1)}), bf16[512,3072]{1,0:T(8,128)(2,1)}) %all-gather.2.cloned.1.call-update) | async-done | bytes 3145744 | tf_op jit(solution)/shard_map/all_gather | solution.py:20
  50.9 436.2 %while.10 = (s32[]{:T(128)}, f32[4,128,128]{2,1,0:T(8,128)S(1)}, f32[4,128,128]{2,1,0:T(8,128)}, s32[]{:T(128)}) while((s32[]{:T(128)}, f32[4,128,128]{2,1,0:T(8,128)S(1)}, f32[4,128,128]{2,1,0:T(8,128)}, s32[]{:T(128)}) %tuple.19), condition=%wide.region_1.0_spmd, body=%wide.region_0.0_spmd.sunk | while | flops 65538 | bytes 1835101 | solution.py:44
  56.0 10.5 %collective-permute-done = f32[4,128,128]{2,1,0:T(8,128)S(1)} collective-permute-done((f32[4,128,128]{2,1,0:T(8,128)}, f32[4,128,128]{2,1,0:T(8,128)S(1)}, u32[]{:S(2)}, u32[]{:S(2)}) %collective-permute-start) | collective-permute-done | bytes 262176 | tf_op jit(solution)/shard_map/while/body/eval_jaxpr/ppermute | solution.py:14
  70.0 11.1 %collective-permute-done = f32[4,128,128]{2,1,0:T(8,128)S(1)} collective-permute-done((f32[4,128,128]{2,1,0:T(8,128)}, f32[4,128,128]{2,1,0:T(8,128)S(1)}, u32[]{:S(2)}, u32[]{:S(2)}) %collective-permute-start) | collective-permute-done | bytes 262176 | tf_op jit(solution)/shard_map/while/body/eval_jaxpr/ppermute | solution.py:14
  84.7 10.2 %collective-permute-done = f32[4,128,128]{2,1,0:T(8,128)S(1)} collective-permute-done((f32[4,128,128]{2,1,0:T(8,128)}, f32[4,128,128]{2,1,0:T(8,128)S(1)}, u32[]{:S(2)}, u32[]{:S(2)}) %collective-permute-start) | collective-permute-done | bytes 262176 | tf_op jit(solution)/shard_map/while/body/eval_jaxpr/ppermute | solution.py:14
  98.5 9.9 %collective-permute-done = f32[4,128,128]{2,1,0:T(8,128)S(1)} collective-permute-done((f32[4,128,128]{2,1,0:T(8,128)}, f32[4,128,128]{2,1,0:T(8,128)S(1)}, u32[]{:S(2)}, u32[]{:S(2)}) %collective-permute-start) | collective-permute-done | bytes 262176 | tf_op jit(solution)/shard_map/while/body/eval_jaxpr/ppermute | solution.py:14
  112.0 9.9 %collective-permute-done = f32[4,128,128]{2,1,0:T(8,128)S(1)} collective-permute-done((f32[4,128,128]{2,1,0:T(8,128)}, f32[4,128,128]{2,1,0:T(8,128)S(1)}, u32[]{:S(2)}, u32[]{:S(2)}) %collective-permute-start) | collective-permute-done | bytes 262176 | tf_op jit(solution)/shard_map/while/body/eval_jaxpr/ppermute | solution.py:14
  165.8 9.9 %collective-permute-done = f32[4,128,128]{2,1,0:T(8,128)S(1)} collective-permute-done((f32[4,128,128]{2,1,0:T(8,128)}, f32[4,128,128]{2,1,0:T(8,128)S(1)}, u32[]{:S(2)}, u32[]{:S(2)}) %collective-permute-start) | collective-permute-done | bytes 262176 | tf_op jit(solution)/shard_map/while/body/eval_jaxpr/ppermute | solution.py:14
  179.3 10.6 %collective-permute-done = f32[4,128,128]{2,1,0:T(8,128)S(1)} collective-permute-done((f32[4,128,128]{2,1,0:T(8,128)}, f32[4,128,128]{2,1,0:T(8,128)S(1)}, u32[]{:S(2)}, u32[]{:S(2)}) %collective-permute-start) | collective-permute-done | bytes 262176 | tf_op jit(solution)/shard_map/while/body/eval_jaxpr/ppermute | solution.py:14
  193.4 11.7 %collective-permute-done = f32[4,128,128]{2,1,0:T(8,128)S(1)} collective-permute-done((f32[4,128,128]{2,1,0:T(8,128)}, f32[4,128,128]{2,1,0:T(8,128)S(1)}, u32[]{:S(2)}, u32[]{:S(2)}) %collective-permute-start) | collective-permute-done | bytes 262176 | tf_op jit(solution)/shard_map/while/body/eval_jaxpr/ppermute | solution.py:14
  208.7 12.5 %collective-permute-done = f32[4,128,128]{2,1,0:T(8,128)S(1)} collective-permute-done((f32[4,128,128]{2,1,0:T(8,128)}, f32[4,128,128]{2,1,0:T(8,128)S(1)}, u32[]{:S(2)}, u32[]{:S(2)}) %collective-permute-start) | collective-permute-done | bytes 262176 | tf_op jit(solution)/shard_map/while/body/eval_jaxpr/ppermute | solution.py:14
  224.8 11.6 %collective-permute-done = f32[4,128,128]{2,1,0:T(8,128)S(1)} collective-permute-done((f32[4,128,128]{2,1,0:T(8,128)}, f32[4,128,128]{2,1,0:T(8,128)S(1)}, u32[]{:S(2)}, u32[]{:S(2)}) %collective-permute-start) | collective-permute-done | bytes 262176 | tf_op jit(solution)/shard_map/while/body/eval_jaxpr/ppermute | solution.py:14
  240.0 10.8 %collective-permute-done = f32[4,128,128]{2,1,0:T(8,128)S(1)} collective-permute-done((f32[4,128,128]{2,1,0:T(8,128)}, f32[4,128,128]{2,1,0:T(8,128)S(1)}, u32[]{:S(2)}, u32[]{:S(2)}) %collective-permute-start) | collective-permute-done | bytes 262176 | tf_op jit(solution)/shard_map/while/body/eval_jaxpr/ppermute | solution.py:14
  254.4 9.9 %collective-permute-done = f32[4,128,128]{2,1,0:T(8,128)S(1)} collective-permute-done((f32[4,128,128]{2,1,0:T(8,128)}, f32[4,128,128]{2,1,0:T(8,128)S(1)}, u32[]{:S(2)}, u32[]{:S(2)}) %collective-permute-start) | collective-permute-done | bytes 262176 | tf_op jit(solution)/shard_map/while/body/eval_jaxpr/ppermute | solution.py:14
  267.9 9.9 %collective-permute-done = f32[4,128,128]{2,1,0:T(8,128)S(1)} collective-permute-done((f32[4,128,128]{2,1,0:T(8,128)}, f32[4,128,128]{2,1,0:T(8,128)S(1)}, u32[]{:S(2)}, u32[]{:S(2)}) %collective-permute-start) | collective-permute-done | bytes 262176 | tf_op jit(solution)/shard_map/while/body/eval_jaxpr/ppermute | solution.py:14
  281.3 9.9 %collective-permute-done = f32[4,128,128]{2,1,0:T(8,128)S(1)} collective-permute-done((f32[4,128,128]{2,1,0:T(8,128)}, f32[4,128,128]{2,1,0:T(8,128)S(1)}, u32[]{:S(2)}, u32[]{:S(2)}) %collective-permute-start) | collective-permute-done | bytes 262176 | tf_op jit(solution)/shard_map/while/body/eval_jaxpr/ppermute | solution.py:14
  294.8 9.9 %collective-permute-done = f32[4,128,128]{2,1,0:T(8,128)S(1)} collective-permute-done((f32[4,128,128]{2,1,0:T(8,128)}, f32[4,128,128]{2,1,0:T(8,128)S(1)}, u32[]{:S(2)}, u32[]{:S(2)}) %collective-permute-start) | collective-permute-done | bytes 262176 | tf_op jit(solution)/shard_map/while/body/eval_jaxpr/ppermute | solution.py:14
  348.6 10.9 %collective-permute-done = f32[4,128,128]{2,1,0:T(8,128)S(1)} collective-permute-done((f32[4,128,128]{2,1,0:T(8,128)}, f32[4,128,128]{2,1,0:T(8,128)S(1)}, u32[]{:S(2)}, u32[]{:S(2)}) %collective-permute-start) | collective-permute-done | bytes 262176 | tf_op jit(solution)/shard_map/while/body/eval_jaxpr/ppermute | solution.py:14
  363.1 12.0 %collective-permute-done = f32[4,128,128]{2,1,0:T(8,128)S(1)} collective-permute-done((f32[4,128,128]{2,1,0:T(8,128)}, f32[4,128,128]{2,1,0:T(8,128)S(1)}, u32[]{:S(2)}, u32[]{:S(2)}) %collective-permute-start) | collective-permute-done | bytes 262176 | tf_op jit(solution)/shard_map/while/body/eval_jaxpr/ppermute | solution.py:14
  378.7 12.2 %collective-permute-done = f32[4,128,128]{2,1,0:T(8,128)S(1)} collective-permute-done((f32[4,128,128]{2,1,0:T(8,128)}, f32[4,128,128]{2,1,0:T(8,128)S(1)}, u32[]{:S(2)}, u32[]{:S(2)}) %collective-permute-start) | collective-permute-done | bytes 262176 | tf_op jit(solution)/shard_map/while/body/eval_jaxpr/ppermute | solution.py:14
  394.5 11.3 %collective-permute-done = f32[4,128,128]{2,1,0:T(8,128)S(1)} collective-permute-done((f32[4,128,128]{2,1,0:T(8,128)}, f32[4,128,128]{2,1,0:T(8,128)S(1)}, u32[]{:S(2)}, u32[]{:S(2)}) %collective-permute-start) | collective-permute-done | bytes 262176 | tf_op jit(solution)/shard_map/while/body/eval_jaxpr/ppermute | solution.py:14
  409.4 10.5 %collective-permute-done = f32[4,128,128]{2,1,0:T(8,128)S(1)} collective-permute-done((f32[4,128,128]{2,1,0:T(8,128)}, f32[4,128,128]{2,1,0:T(8,128)S(1)}, u32[]{:S(2)}, u32[]{:S(2)}) %collective-permute-start) | collective-permute-done | bytes 262176 | tf_op jit(solution)/shard_map/while/body/eval_jaxpr/ppermute | solution.py:14
  463.8 9.9 %collective-permute-done = f32[4,128,128]{2,1,0:T(8,128)S(1)} collective-permute-done((f32[4,128,128]{2,1,0:T(8,128)}, f32[4,128,128]{2,1,0:T(8,128)S(1)}, u32[]{:S(2)}, u32[]{:S(2)}) %collective-permute-start) | collective-permute-done | bytes 262176 | tf_op jit(solution)/shard_map/while/body/eval_jaxpr/ppermute | solution.py:14
  477.3 9.9 %collective-permute-done = f32[4,128,128]{2,1,0:T(8,128)S(1)} collective-permute-done((f32[4,128,128]{2,1,0:T(8,128)}, f32[4,128,128]{2,1,0:T(8,128)S(1)}, u32[]{:S(2)}, u32[]{:S(2)}) %collective-permute-start) | collective-permute-done | bytes 262176 | tf_op jit(solution)/shard_map/while/body/eval_jaxpr/ppermute | solution.py:14
  (97 shorter events, 223.5 us)
Async XLA Ops:
  6.5 34.4 %all-gather.2.cloned.1.call-start = ((), (), s32[]{:S(2)}) async-start(), calls=%async_computation | async-start | bytes 3538944 | tf_op jit(solution)/shard_map/all_gather | solution.py:20
  52.6 13.9 %collective-permute-start = (f32[4,128,128]{2,1,0:T(8,128)}, f32[4,128,128]{2,1,0:T(8,128)S(1)}, u32[]{:S(2)}, u32[]{:S(2)}) collective-permute-start(f32[4,128,128]{2,1,0:T(8,128)} %add.39), channel_id=1, source_target_pairs={{0,8},{8,16},{16,24},{24,32},{32,40},{40,48},{48,56},{56,64},{64,7... | collective-permute-start | bytes 786440 | tf_op jit(solution)/shard_map/while/body/eval_jaxpr/ppermute | solution.py:14
  68.1 13.0 %collective-permute-start = (f32[4,128,128]{2,1,0:T(8,128)}, f32[4,128,128]{2,1,0:T(8,128)S(1)}, u32[]{:S(2)}, u32[]{:S(2)}) collective-permute-start(f32[4,128,128]{2,1,0:T(8,128)} %add.39), channel_id=1, source_target_pairs={{0,8},{8,16},{16,24},{24,32},{32,40},{40,48},{48,56},{56,64},{64,7... | collective-permute-start | bytes 786440 | tf_op jit(solution)/shard_map/while/body/eval_jaxpr/ppermute | solution.py:14
  82.8 12.1 %collective-permute-start = (f32[4,128,128]{2,1,0:T(8,128)}, f32[4,128,128]{2,1,0:T(8,128)S(1)}, u32[]{:S(2)}, u32[]{:S(2)}) collective-permute-start(f32[4,128,128]{2,1,0:T(8,128)} %add.39), channel_id=1, source_target_pairs={{0,8},{8,16},{16,24},{24,32},{32,40},{40,48},{48,56},{56,64},{64,7... | collective-permute-start | bytes 786440 | tf_op jit(solution)/shard_map/while/body/eval_jaxpr/ppermute | solution.py:14
  96.6 11.8 %collective-permute-start = (f32[4,128,128]{2,1,0:T(8,128)}, f32[4,128,128]{2,1,0:T(8,128)S(1)}, u32[]{:S(2)}, u32[]{:S(2)}) collective-permute-start(f32[4,128,128]{2,1,0:T(8,128)} %add.39), channel_id=1, source_target_pairs={{0,8},{8,16},{16,24},{24,32},{32,40},{40,48},{48,56},{56,64},{64,7... | collective-permute-start | bytes 786440 | tf_op jit(solution)/shard_map/while/body/eval_jaxpr/ppermute | solution.py:14
  110.1 11.8 %collective-permute-start = (f32[4,128,128]{2,1,0:T(8,128)}, f32[4,128,128]{2,1,0:T(8,128)S(1)}, u32[]{:S(2)}, u32[]{:S(2)}) collective-permute-start(f32[4,128,128]{2,1,0:T(8,128)} %add.39), channel_id=1, source_target_pairs={{0,8},{8,16},{16,24},{24,32},{32,40},{40,48},{48,56},{56,64},{64,7... | collective-permute-start | bytes 786440 | tf_op jit(solution)/shard_map/while/body/eval_jaxpr/ppermute | solution.py:14
  123.5 11.8 %collective-permute-start = (f32[4,128,128]{2,1,0:T(8,128)}, f32[4,128,128]{2,1,0:T(8,128)S(1)}, u32[]{:S(2)}, u32[]{:S(2)}) collective-permute-start(f32[4,128,128]{2,1,0:T(8,128)} %add.39), channel_id=1, source_target_pairs={{0,8},{8,16},{16,24},{24,32},{32,40},{40,48},{48,56},{56,64},{64,7... | collective-permute-start | bytes 786440 | tf_op jit(solution)/shard_map/while/body/eval_jaxpr/ppermute | solution.py:14
  137.0 11.8 %collective-permute-start = (f32[4,128,128]{2,1,0:T(8,128)}, f32[4,128,128]{2,1,0:T(8,128)S(1)}, u32[]{:S(2)}, u32[]{:S(2)}) collective-permute-start(f32[4,128,128]{2,1,0:T(8,128)} %add.39), channel_id=1, source_target_pairs={{0,8},{8,16},{16,24},{24,32},{32,40},{40,48},{48,56},{56,64},{64,7... | collective-permute-start | bytes 786440 | tf_op jit(solution)/shard_map/while/body/eval_jaxpr/ppermute | solution.py:14
  150.4 11.8 %collective-permute-start = (f32[4,128,128]{2,1,0:T(8,128)}, f32[4,128,128]{2,1,0:T(8,128)S(1)}, u32[]{:S(2)}, u32[]{:S(2)}) collective-permute-start(f32[4,128,128]{2,1,0:T(8,128)} %add.39), channel_id=1, source_target_pairs={{0,8},{8,16},{16,24},{24,32},{32,40},{40,48},{48,56},{56,64},{64,7... | collective-permute-start | bytes 786440 | tf_op jit(solution)/shard_map/while/body/eval_jaxpr/ppermute | solution.py:14
  163.9 11.8 %collective-permute-start = (f32[4,128,128]{2,1,0:T(8,128)}, f32[4,128,128]{2,1,0:T(8,128)S(1)}, u32[]{:S(2)}, u32[]{:S(2)}) collective-permute-start(f32[4,128,128]{2,1,0:T(8,128)} %add.39), channel_id=1, source_target_pairs={{0,8},{8,16},{16,24},{24,32},{32,40},{40,48},{48,56},{56,64},{64,7... | collective-permute-start | bytes 786440 | tf_op jit(solution)/shard_map/while/body/eval_jaxpr/ppermute | solution.py:14
  177.3 12.5 %collective-permute-start = (f32[4,128,128]{2,1,0:T(8,128)}, f32[4,128,128]{2,1,0:T(8,128)S(1)}, u32[]{:S(2)}, u32[]{:S(2)}) collective-permute-start(f32[4,128,128]{2,1,0:T(8,128)} %add.39), channel_id=1, source_target_pairs={{0,8},{8,16},{16,24},{24,32},{32,40},{40,48},{48,56},{56,64},{64,7... | collective-permute-start | bytes 786440 | tf_op jit(solution)/shard_map/while/body/eval_jaxpr/ppermute | solution.py:14
  191.5 13.6 %collective-permute-start = (f32[4,128,128]{2,1,0:T(8,128)}, f32[4,128,128]{2,1,0:T(8,128)S(1)}, u32[]{:S(2)}, u32[]{:S(2)}) collective-permute-start(f32[4,128,128]{2,1,0:T(8,128)} %add.39), channel_id=1, source_target_pairs={{0,8},{8,16},{16,24},{24,32},{32,40},{40,48},{48,56},{56,64},{64,7... | collective-permute-start | bytes 786440 | tf_op jit(solution)/shard_map/while/body/eval_jaxpr/ppermute | solution.py:14
  206.8 14.4 %collective-permute-start = (f32[4,128,128]{2,1,0:T(8,128)}, f32[4,128,128]{2,1,0:T(8,128)S(1)}, u32[]{:S(2)}, u32[]{:S(2)}) collective-permute-start(f32[4,128,128]{2,1,0:T(8,128)} %add.39), channel_id=1, source_target_pairs={{0,8},{8,16},{16,24},{24,32},{32,40},{40,48},{48,56},{56,64},{64,7... | collective-permute-start | bytes 786440 | tf_op jit(solution)/shard_map/while/body/eval_jaxpr/ppermute | solution.py:14
  222.9 13.6 %collective-permute-start = (f32[4,128,128]{2,1,0:T(8,128)}, f32[4,128,128]{2,1,0:T(8,128)S(1)}, u32[]{:S(2)}, u32[]{:S(2)}) collective-permute-start(f32[4,128,128]{2,1,0:T(8,128)} %add.39), channel_id=1, source_target_pairs={{0,8},{8,16},{16,24},{24,32},{32,40},{40,48},{48,56},{56,64},{64,7... | collective-permute-start | bytes 786440 | tf_op jit(solution)/shard_map/while/body/eval_jaxpr/ppermute | solution.py:14
  238.1 12.7 %collective-permute-start = (f32[4,128,128]{2,1,0:T(8,128)}, f32[4,128,128]{2,1,0:T(8,128)S(1)}, u32[]{:S(2)}, u32[]{:S(2)}) collective-permute-start(f32[4,128,128]{2,1,0:T(8,128)} %add.39), channel_id=1, source_target_pairs={{0,8},{8,16},{16,24},{24,32},{32,40},{40,48},{48,56},{56,64},{64,7... | collective-permute-start | bytes 786440 | tf_op jit(solution)/shard_map/while/body/eval_jaxpr/ppermute | solution.py:14
  252.5 11.8 %collective-permute-start = (f32[4,128,128]{2,1,0:T(8,128)}, f32[4,128,128]{2,1,0:T(8,128)S(1)}, u32[]{:S(2)}, u32[]{:S(2)}) collective-permute-start(f32[4,128,128]{2,1,0:T(8,128)} %add.39), channel_id=1, source_target_pairs={{0,8},{8,16},{16,24},{24,32},{32,40},{40,48},{48,56},{56,64},{64,7... | collective-permute-start | bytes 786440 | tf_op jit(solution)/shard_map/while/body/eval_jaxpr/ppermute | solution.py:14
  266.0 11.8 %collective-permute-start = (f32[4,128,128]{2,1,0:T(8,128)}, f32[4,128,128]{2,1,0:T(8,128)S(1)}, u32[]{:S(2)}, u32[]{:S(2)}) collective-permute-start(f32[4,128,128]{2,1,0:T(8,128)} %add.39), channel_id=1, source_target_pairs={{0,8},{8,16},{16,24},{24,32},{32,40},{40,48},{48,56},{56,64},{64,7... | collective-permute-start | bytes 786440 | tf_op jit(solution)/shard_map/while/body/eval_jaxpr/ppermute | solution.py:14
  279.4 11.8 %collective-permute-start = (f32[4,128,128]{2,1,0:T(8,128)}, f32[4,128,128]{2,1,0:T(8,128)S(1)}, u32[]{:S(2)}, u32[]{:S(2)}) collective-permute-start(f32[4,128,128]{2,1,0:T(8,128)} %add.39), channel_id=1, source_target_pairs={{0,8},{8,16},{16,24},{24,32},{32,40},{40,48},{48,56},{56,64},{64,7... | collective-permute-start | bytes 786440 | tf_op jit(solution)/shard_map/while/body/eval_jaxpr/ppermute | solution.py:14
  346.7 12.8 %collective-permute-start = (f32[4,128,128]{2,1,0:T(8,128)}, f32[4,128,128]{2,1,0:T(8,128)S(1)}, u32[]{:S(2)}, u32[]{:S(2)}) collective-permute-start(f32[4,128,128]{2,1,0:T(8,128)} %add.39), channel_id=1, source_target_pairs={{0,8},{8,16},{16,24},{24,32},{32,40},{40,48},{48,56},{56,64},{64,7... | collective-permute-start | bytes 786440 | tf_op jit(solution)/shard_map/while/body/eval_jaxpr/ppermute | solution.py:14
  361.2 13.9 %collective-permute-start = (f32[4,128,128]{2,1,0:T(8,128)}, f32[4,128,128]{2,1,0:T(8,128)S(1)}, u32[]{:S(2)}, u32[]{:S(2)}) collective-permute-start(f32[4,128,128]{2,1,0:T(8,128)} %add.39), channel_id=1, source_target_pairs={{0,8},{8,16},{16,24},{24,32},{32,40},{40,48},{48,56},{56,64},{64,7... | collective-permute-start | bytes 786440 | tf_op jit(solution)/shard_map/while/body/eval_jaxpr/ppermute | solution.py:14
  376.8 14.1 %collective-permute-start = (f32[4,128,128]{2,1,0:T(8,128)}, f32[4,128,128]{2,1,0:T(8,128)S(1)}, u32[]{:S(2)}, u32[]{:S(2)}) collective-permute-start(f32[4,128,128]{2,1,0:T(8,128)} %add.39), channel_id=1, source_target_pairs={{0,8},{8,16},{16,24},{24,32},{32,40},{40,48},{48,56},{56,64},{64,7... | collective-permute-start | bytes 786440 | tf_op jit(solution)/shard_map/while/body/eval_jaxpr/ppermute | solution.py:14
  392.5 13.2 %collective-permute-start = (f32[4,128,128]{2,1,0:T(8,128)}, f32[4,128,128]{2,1,0:T(8,128)S(1)}, u32[]{:S(2)}, u32[]{:S(2)}) collective-permute-start(f32[4,128,128]{2,1,0:T(8,128)} %add.39), channel_id=1, source_target_pairs={{0,8},{8,16},{16,24},{24,32},{32,40},{40,48},{48,56},{56,64},{64,7... | collective-permute-start | bytes 786440 | tf_op jit(solution)/shard_map/while/body/eval_jaxpr/ppermute | solution.py:14
  407.5 12.4 %collective-permute-start = (f32[4,128,128]{2,1,0:T(8,128)}, f32[4,128,128]{2,1,0:T(8,128)S(1)}, u32[]{:S(2)}, u32[]{:S(2)}) collective-permute-start(f32[4,128,128]{2,1,0:T(8,128)} %add.39), channel_id=1, source_target_pairs={{0,8},{8,16},{16,24},{24,32},{32,40},{40,48},{48,56},{56,64},{64,7... | collective-permute-start | bytes 786440 | tf_op jit(solution)/shard_map/while/body/eval_jaxpr/ppermute | solution.py:14
  461.9 11.8 %collective-permute-start = (f32[4,128,128]{2,1,0:T(8,128)}, f32[4,128,128]{2,1,0:T(8,128)S(1)}, u32[]{:S(2)}, u32[]{:S(2)}) collective-permute-start(f32[4,128,128]{2,1,0:T(8,128)} %add.39), channel_id=1, source_target_pairs={{0,8},{8,16},{16,24},{24,32},{32,40},{40,48},{48,56},{56,64},{64,7... | collective-permute-start | bytes 786440 | tf_op jit(solution)/shard_map/while/body/eval_jaxpr/ppermute | solution.py:14
  (14 other events, 143.7 us)
Sparse Core Ops, SparseCore 0:
  9.2 31.7 all-gather.1
where the time goes:
time: 507 us; the launch traced here: 505 us
  waiting for transfers between devices  357 us (70%)
  starting transfers between devices  60.6 us (12%)
  other arithmetic  54.9 us (11%)
  matrix products  15.3 us (3%)
  between operations  13.5 us (3%)
    ppermute x31, waiting for transfers between devices, from_behind(): return lax.ppermute(value, axis, pairs)  323 us
    ppermute x31, starting transfers between devices, from_behind(): return lax.ppermute(value, axis, pairs)  60.6 us
    add x31, other arithmetic, advance(): return from_behind(carried + local_state, 'ctx', 1)  51.8 us
    all_gather x1, waiting for transfers between devices, body(): piece_rows = lax.all_gather(tokens, 'tp', axis=0, tiled=True)  32.9 us
  transfers between devices with their start and end apart: 32, of which 32 were waited for; matrix products, arithmetic and copies ran while one was open for 0% of the time, Pallas kernels for 0%

commit v1 on v0

--- a/solution.py
+++ b/solution.py
@@ -17,7 +17,22 @@
 def body(tokens, w_query, w_key, w_value, norm_gain):
     local_width = w_query.shape[1]
     head_count = local_width // HEAD_DIM
-    piece_rows = lax.all_gather(tokens, "tp", axis=0, tiled=True)
+    peers, index, rows = (lax.axis_size("tp"), lax.axis_index("tp"), tokens.shape[0])
+    right = [(i_2, (i_2 + 1) % peers) for i_2 in range(peers)]
+    left = [(i_2, (i_2 - 1) % peers) for i_2 in range(peers)]
+    out = jnp.zeros((*tokens.shape[:0], peers * rows, *tokens.shape[0 + 1 :]), tokens.dtype)
+    out = lax.dynamic_update_slice_in_dim(out, tokens, index * rows, axis=0)
+    from_left = from_right = tokens
+    half = peers // 2
+    for step in range(1, half + 1):
+        from_left = lax.ppermute(from_left, "tp", right)
+        out = lax.dynamic_update_slice_in_dim(out, from_left, (index - step) % peers * rows, axis=0)
+        if step < peers - half:
+            from_right = lax.ppermute(from_right, "tp", left)
+            out = lax.dynamic_update_slice_in_dim(
+                out, from_right, (index + step) % peers * rows, axis=0
+            )
+    piece_rows = out
     query_part = jnp.dot(piece_rows, w_query, preferred_element_type=jnp.float32).astype(
         jnp.bfloat16
     )

time: 507 us -> 491 us (0.968)
  between operations: 13.5 us -> 0.16 us
  waiting for transfers between devices: 357 us -> 344 us
  starting transfers between devices: 60.6 us -> 69.5 us
    all_gather x1 -> x0, waiting for transfers between devices: 32.9 us -> none  [body(): piece_rows = lax.all_gather(tokens, 'tp', axis=0, tiled=True)]
    ppermute x0 -> x7, waiting for transfers between devices: none -> 21.9 us  [the longest x4 21.9 us: body(): from_left = lax.ppermute(from_left, 'tp', right)]
    ppermute x0 -> x7, starting transfers between devices: none -> 8.87 us  [the longest x3 8.86 us: body(): from_right = lax.ppermute(from_right, 'tp', left)]
  transfers between devices with their start and end apart: 32 -> 38, of which waited for: 32 -> 35; matrix products, arithmetic and copies ran while one was open for 0% -> 1% of each run, Pallas kernels for 0% -> 0%
where the time goes in v1:
time: 491 us; the launch traced here: 488 us
  waiting for transfers between devices  344 us (70%)
  starting transfers between devices  69.5 us (14%)
  other arithmetic  55.2 us (11%)
  matrix products  13.3 us (3%)
  local copies, waits for them, and re-layouts  5.9 us (1%)
    ppermute x31, waiting for transfers between devices, from_behind(): return lax.ppermute(value, axis, pairs)  322 us
    ppermute x31, starting transfers between devices, from_behind(): return lax.ppermute(value, axis, pairs)  60.6 us
    add x31, other arithmetic, advance(): return from_behind(carried + local_state, 'ctx', 1)  52.1 us
    ppermute x4, waiting for transfers between devices, body(): from_left = lax.ppermute(from_left, 'tp', right)  21.9 us
  transfers between devices with their start and end apart: 38, of which 35 were waited for; matrix products, arithmetic and copies ran while one was open for 1% of the time, Pallas kernels for 0%

profile of v1, /device:TPU:128, one launch (start us, length us, event | category | flops | bytes accessed | tf_op | source)
XLA Modules:
  0.0 488.3 jit_solution(6461197437324007264)
XLA Ops:
  42.1 435.1 %while.10 = (s32[]{:T(128)}, f32[4,128,128]{2,1,0:T(8,128)S(1)}, f32[4,128,128]{2,1,0:T(8,128)}, s32[]{:T(128)}) while((s32[]{:T(128)}, f32[4,128,128]{2,1,0:T(8,128)S(1)}, f32[4,128,128]{2,1,0:T(8,128)}, s32[]{:T(128)}) %tuple.19), condition=%wide.region_1.2_spmd, body=%wide.region_0.1_spmd.sunk | while | flops 65538 | bytes 1835101 | solution.py:59
  59.2 9.9 %collective-permute-done = f32[4,128,128]{2,1,0:T(8,128)S(1)} collective-permute-done((f32[4,128,128]{2,1,0:T(8,128)}, f32[4,128,128]{2,1,0:T(8,128)S(1)}, u32[]{:S(2)}, u32[]{:S(2)}) %collective-permute-start) | collective-permute-done | bytes 262176 | tf_op jit(solution)/shard_map/while/body/eval_jaxpr/ppermute | solution.py:14
  72.7 9.9 %collective-permute-done = f32[4,128,128]{2,1,0:T(8,128)S(1)} collective-permute-done((f32[4,128,128]{2,1,0:T(8,128)}, f32[4,128,128]{2,1,0:T(8,128)S(1)}, u32[]{:S(2)}, u32[]{:S(2)}) %collective-permute-start) | collective-permute-done | bytes 262176 | tf_op jit(solution)/shard_map/while/body/eval_jaxpr/ppermute | solution.py:14
  86.2 10.4 %collective-permute-done = f32[4,128,128]{2,1,0:T(8,128)S(1)} collective-permute-done((f32[4,128,128]{2,1,0:T(8,128)}, f32[4,128,128]{2,1,0:T(8,128)S(1)}, u32[]{:S(2)}, u32[]{:S(2)}) %collective-permute-start) | collective-permute-done | bytes 262176 | tf_op jit(solution)/shard_map/while/body/eval_jaxpr/ppermute | solution.py:14
  100.2 11.5 %collective-permute-done = f32[4,128,128]{2,1,0:T(8,128)S(1)} collective-permute-done((f32[4,128,128]{2,1,0:T(8,128)}, f32[4,128,128]{2,1,0:T(8,128)S(1)}, u32[]{:S(2)}, u32[]{:S(2)}) %collective-permute-start) | collective-permute-done | bytes 262176 | tf_op jit(solution)/shard_map/while/body/eval_jaxpr/ppermute | solution.py:14
  115.3 12.6 %collective-permute-done = f32[4,128,128]{2,1,0:T(8,128)S(1)} collective-permute-done((f32[4,128,128]{2,1,0:T(8,128)}, f32[4,128,128]{2,1,0:T(8,128)S(1)}, u32[]{:S(2)}, u32[]{:S(2)}) %collective-permute-start) | collective-permute-done | bytes 262176 | tf_op jit(solution)/shard_map/while/body/eval_jaxpr/ppermute | solution.py:14
  131.6 11.8 %collective-permute-done = f32[4,128,128]{2,1,0:T(8,128)S(1)} collective-permute-done((f32[4,128,128]{2,1,0:T(8,128)}, f32[4,128,128]{2,1,0:T(8,128)S(1)}, u32[]{:S(2)}, u32[]{:S(2)}) %collective-permute-start) | collective-permute-done | bytes 262176 | tf_op jit(solution)/shard_map/while/body/eval_jaxpr/ppermute | solution.py:14
  147.0 10.9 %collective-permute-done = f32[4,128,128]{2,1,0:T(8,128)S(1)} collective-permute-done((f32[4,128,128]{2,1,0:T(8,128)}, f32[4,128,128]{2,1,0:T(8,128)S(1)}, u32[]{:S(2)}, u32[]{:S(2)}) %collective-permute-start) | collective-permute-done | bytes 262176 | tf_op jit(solution)/shard_map/while/body/eval_jaxpr/ppermute | solution.py:14
  161.5 10.1 %collective-permute-done = f32[4,128,128]{2,1,0:T(8,128)S(1)} collective-permute-done((f32[4,128,128]{2,1,0:T(8,128)}, f32[4,128,128]{2,1,0:T(8,128)S(1)}, u32[]{:S(2)}, u32[]{:S(2)}) %collective-permute-start) | collective-permute-done | bytes 262176 | tf_op jit(solution)/shard_map/while/body/eval_jaxpr/ppermute | solution.py:14
  175.2 9.9 %collective-permute-done = f32[4,128,128]{2,1,0:T(8,128)S(1)} collective-permute-done((f32[4,128,128]{2,1,0:T(8,128)}, f32[4,128,128]{2,1,0:T(8,128)S(1)}, u32[]{:S(2)}, u32[]{:S(2)}) %collective-permute-start) | collective-permute-done | bytes 262176 | tf_op jit(solution)/shard_map/while/body/eval_jaxpr/ppermute | solution.py:14
  188.6 9.9 %collective-permute-done = f32[4,128,128]{2,1,0:T(8,128)S(1)} collective-permute-done((f32[4,128,128]{2,1,0:T(8,128)}, f32[4,128,128]{2,1,0:T(8,128)S(1)}, u32[]{:S(2)}, u32[]{:S(2)}) %collective-permute-start) | collective-permute-done | bytes 262176 | tf_op jit(solution)/shard_map/while/body/eval_jaxpr/ppermute | solution.py:14
  229.0 9.9 %collective-permute-done = f32[4,128,128]{2,1,0:T(8,128)S(1)} collective-permute-done((f32[4,128,128]{2,1,0:T(8,128)}, f32[4,128,128]{2,1,0:T(8,128)S(1)}, u32[]{:S(2)}, u32[]{:S(2)}) %collective-permute-start) | collective-permute-done | bytes 262176 | tf_op jit(solution)/shard_map/while/body/eval_jaxpr/ppermute | solution.py:14
  242.5 9.9 %collective-permute-done = f32[4,128,128]{2,1,0:T(8,128)S(1)} collective-permute-done((f32[4,128,128]{2,1,0:T(8,128)}, f32[4,128,128]{2,1,0:T(8,128)S(1)}, u32[]{:S(2)}, u32[]{:S(2)}) %collective-permute-start) | collective-permute-done | bytes 262176 | tf_op jit(solution)/shard_map/while/body/eval_jaxpr/ppermute | solution.py:14
  256.0 10.7 %collective-permute-done = f32[4,128,128]{2,1,0:T(8,128)S(1)} collective-permute-done((f32[4,128,128]{2,1,0:T(8,128)}, f32[4,128,128]{2,1,0:T(8,128)S(1)}, u32[]{:S(2)}, u32[]{:S(2)}) %collective-permute-start) | collective-permute-done | bytes 262176 | tf_op jit(solution)/shard_map/while/body/eval_jaxpr/ppermute | solution.py:14
  270.3 11.8 %collective-permute-done = f32[4,128,128]{2,1,0:T(8,128)S(1)} collective-permute-done((f32[4,128,128]{2,1,0:T(8,128)}, f32[4,128,128]{2,1,0:T(8,128)S(1)}, u32[]{:S(2)}, u32[]{:S(2)}) %collective-permute-start) | collective-permute-done | bytes 262176 | tf_op jit(solution)/shard_map/while/body/eval_jaxpr/ppermute | solution.py:14
  285.7 12.4 %collective-permute-done = f32[4,128,128]{2,1,0:T(8,128)S(1)} collective-permute-done((f32[4,128,128]{2,1,0:T(8,128)}, f32[4,128,128]{2,1,0:T(8,128)S(1)}, u32[]{:S(2)}, u32[]{:S(2)}) %collective-permute-start) | collective-permute-done | bytes 262176 | tf_op jit(solution)/shard_map/while/body/eval_jaxpr/ppermute | solution.py:14
  301.7 11.5 %collective-permute-done = f32[4,128,128]{2,1,0:T(8,128)S(1)} collective-permute-done((f32[4,128,128]{2,1,0:T(8,128)}, f32[4,128,128]{2,1,0:T(8,128)S(1)}, u32[]{:S(2)}, u32[]{:S(2)}) %collective-permute-start) | collective-permute-done | bytes 262176 | tf_op jit(solution)/shard_map/while/body/eval_jaxpr/ppermute | solution.py:14
  316.8 10.6 %collective-permute-done = f32[4,128,128]{2,1,0:T(8,128)S(1)} collective-permute-done((f32[4,128,128]{2,1,0:T(8,128)}, f32[4,128,128]{2,1,0:T(8,128)S(1)}, u32[]{:S(2)}, u32[]{:S(2)}) %collective-permute-start) | collective-permute-done | bytes 262176 | tf_op jit(solution)/shard_map/while/body/eval_jaxpr/ppermute | solution.py:14
  344.5 9.9 %collective-permute-done = f32[4,128,128]{2,1,0:T(8,128)S(1)} collective-permute-done((f32[4,128,128]{2,1,0:T(8,128)}, f32[4,128,128]{2,1,0:T(8,128)S(1)}, u32[]{:S(2)}, u32[]{:S(2)}) %collective-permute-start) | collective-permute-done | bytes 262176 | tf_op jit(solution)/shard_map/while/body/eval_jaxpr/ppermute | solution.py:14
  357.9 9.9 %collective-permute-done = f32[4,128,128]{2,1,0:T(8,128)S(1)} collective-permute-done((f32[4,128,128]{2,1,0:T(8,128)}, f32[4,128,128]{2,1,0:T(8,128)S(1)}, u32[]{:S(2)}, u32[]{:S(2)}) %collective-permute-start) | collective-permute-done | bytes 262176 | tf_op jit(solution)/shard_map/while/body/eval_jaxpr/ppermute | solution.py:14
  371.4 9.9 %collective-permute-done = f32[4,128,128]{2,1,0:T(8,128)S(1)} collective-permute-done((f32[4,128,128]{2,1,0:T(8,128)}, f32[4,128,128]{2,1,0:T(8,128)S(1)}, u32[]{:S(2)}, u32[]{:S(2)}) %collective-permute-start) | collective-permute-done | bytes 262176 | tf_op jit(solution)/shard_map/while/body/eval_jaxpr/ppermute | solution.py:14
  411.8 10.1 %collective-permute-done = f32[4,128,128]{2,1,0:T(8,128)S(1)} collective-permute-done((f32[4,128,128]{2,1,0:T(8,128)}, f32[4,128,128]{2,1,0:T(8,128)S(1)}, u32[]{:S(2)}, u32[]{:S(2)}) %collective-permute-start) | collective-permute-done | bytes 262176 | tf_op jit(solution)/shard_map/while/body/eval_jaxpr/ppermute | solution.py:14
  425.6 11.3 %collective-permute-done = f32[4,128,128]{2,1,0:T(8,128)S(1)} collective-permute-done((f32[4,128,128]{2,1,0:T(8,128)}, f32[4,128,128]{2,1,0:T(8,128)S(1)}, u32[]{:S(2)}, u32[]{:S(2)}) %collective-permute-start) | collective-permute-done | bytes 262176 | tf_op jit(solution)/shard_map/while/body/eval_jaxpr/ppermute | solution.py:14
  440.4 9.9 %collective-permute-done = f32[4,128,128]{2,1,0:T(8,128)S(1)} collective-permute-done((f32[4,128,128]{2,1,0:T(8,128)}, f32[4,128,128]{2,1,0:T(8,128)S(1)}, u32[]{:S(2)}, u32[]{:S(2)}) %collective-permute-start) | collective-permute-done | bytes 262176 | tf_op jit(solution)/shard_map/while/body/eval_jaxpr/ppermute | solution.py:14
  (117 shorter events, 243.2 us)
Async XLA Ops:
  43.8 11.8 %collective-permute-start = (f32[4,128,128]{2,1,0:T(8,128)}, f32[4,128,128]{2,1,0:T(8,128)S(1)}, u32[]{:S(2)}, u32[]{:S(2)}) collective-permute-start(f32[4,128,128]{2,1,0:T(8,128)} %add.116), channel_id=1, source_target_pairs={{0,8},{8,16},{16,24},{24,32},{32,40},{40,48},{48,56},{56,64},{64,7... | collective-permute-start | bytes 786440 | tf_op jit(solution)/shard_map/while/body/eval_jaxpr/ppermute | solution.py:14
  57.3 11.8 %collective-permute-start = (f32[4,128,128]{2,1,0:T(8,128)}, f32[4,128,128]{2,1,0:T(8,128)S(1)}, u32[]{:S(2)}, u32[]{:S(2)}) collective-permute-start(f32[4,128,128]{2,1,0:T(8,128)} %add.116), channel_id=1, source_target_pairs={{0,8},{8,16},{16,24},{24,32},{32,40},{40,48},{48,56},{56,64},{64,7... | collective-permute-start | bytes 786440 | tf_op jit(solution)/shard_map/while/body/eval_jaxpr/ppermute | solution.py:14
  70.8 11.8 %collective-permute-start = (f32[4,128,128]{2,1,0:T(8,128)}, f32[4,128,128]{2,1,0:T(8,128)S(1)}, u32[]{:S(2)}, u32[]{:S(2)}) collective-permute-start(f32[4,128,128]{2,1,0:T(8,128)} %add.116), channel_id=1, source_target_pairs={{0,8},{8,16},{16,24},{24,32},{32,40},{40,48},{48,56},{56,64},{64,7... | collective-permute-start | bytes 786440 | tf_op jit(solution)/shard_map/while/body/eval_jaxpr/ppermute | solution.py:14
  84.2 12.3 %collective-permute-start = (f32[4,128,128]{2,1,0:T(8,128)}, f32[4,128,128]{2,1,0:T(8,128)S(1)}, u32[]{:S(2)}, u32[]{:S(2)}) collective-permute-start(f32[4,128,128]{2,1,0:T(8,128)} %add.116), channel_id=1, source_target_pairs={{0,8},{8,16},{16,24},{24,32},{32,40},{40,48},{48,56},{56,64},{64,7... | collective-permute-start | bytes 786440 | tf_op jit(solution)/shard_map/while/body/eval_jaxpr/ppermute | solution.py:14
  98.2 13.5 %collective-permute-start = (f32[4,128,128]{2,1,0:T(8,128)}, f32[4,128,128]{2,1,0:T(8,128)S(1)}, u32[]{:S(2)}, u32[]{:S(2)}) collective-permute-start(f32[4,128,128]{2,1,0:T(8,128)} %add.116), channel_id=1, source_target_pairs={{0,8},{8,16},{16,24},{24,32},{32,40},{40,48},{48,56},{56,64},{64,7... | collective-permute-start | bytes 786440 | tf_op jit(solution)/shard_map/while/body/eval_jaxpr/ppermute | solution.py:14
  113.4 14.6 %collective-permute-start = (f32[4,128,128]{2,1,0:T(8,128)}, f32[4,128,128]{2,1,0:T(8,128)S(1)}, u32[]{:S(2)}, u32[]{:S(2)}) collective-permute-start(f32[4,128,128]{2,1,0:T(8,128)} %add.116), channel_id=1, source_target_pairs={{0,8},{8,16},{16,24},{24,32},{32,40},{40,48},{48,56},{56,64},{64,7... | collective-permute-start | bytes 786440 | tf_op jit(solution)/shard_map/while/body/eval_jaxpr/ppermute | solution.py:14
  129.6 13.7 %collective-permute-start = (f32[4,128,128]{2,1,0:T(8,128)}, f32[4,128,128]{2,1,0:T(8,128)S(1)}, u32[]{:S(2)}, u32[]{:S(2)}) collective-permute-start(f32[4,128,128]{2,1,0:T(8,128)} %add.116), channel_id=1, source_target_pairs={{0,8},{8,16},{16,24},{24,32},{32,40},{40,48},{48,56},{56,64},{64,7... | collective-permute-start | bytes 786440 | tf_op jit(solution)/shard_map/while/body/eval_jaxpr/ppermute | solution.py:14
  145.0 12.9 %collective-permute-start = (f32[4,128,128]{2,1,0:T(8,128)}, f32[4,128,128]{2,1,0:T(8,128)S(1)}, u32[]{:S(2)}, u32[]{:S(2)}) collective-permute-start(f32[4,128,128]{2,1,0:T(8,128)} %add.116), channel_id=1, source_target_pairs={{0,8},{8,16},{16,24},{24,32},{32,40},{40,48},{48,56},{56,64},{64,7... | collective-permute-start | bytes 786440 | tf_op jit(solution)/shard_map/while/body/eval_jaxpr/ppermute | solution.py:14
  159.6 12.0 %collective-permute-start = (f32[4,128,128]{2,1,0:T(8,128)}, f32[4,128,128]{2,1,0:T(8,128)S(1)}, u32[]{:S(2)}, u32[]{:S(2)}) collective-permute-start(f32[4,128,128]{2,1,0:T(8,128)} %add.116), channel_id=1, source_target_pairs={{0,8},{8,16},{16,24},{24,32},{32,40},{40,48},{48,56},{56,64},{64,7... | collective-permute-start | bytes 786440 | tf_op jit(solution)/shard_map/while/body/eval_jaxpr/ppermute | solution.py:14
  173.3 11.8 %collective-permute-start = (f32[4,128,128]{2,1,0:T(8,128)}, f32[4,128,128]{2,1,0:T(8,128)S(1)}, u32[]{:S(2)}, u32[]{:S(2)}) collective-permute-start(f32[4,128,128]{2,1,0:T(8,128)} %add.116), channel_id=1, source_target_pairs={{0,8},{8,16},{16,24},{24,32},{32,40},{40,48},{48,56},{56,64},{64,7... | collective-permute-start | bytes 786440 | tf_op jit(solution)/shard_map/while/body/eval_jaxpr/ppermute | solution.py:14
  186.7 11.8 %collective-permute-start = (f32[4,128,128]{2,1,0:T(8,128)}, f32[4,128,128]{2,1,0:T(8,128)S(1)}, u32[]{:S(2)}, u32[]{:S(2)}) collective-permute-start(f32[4,128,128]{2,1,0:T(8,128)} %add.116), channel_id=1, source_target_pairs={{0,8},{8,16},{16,24},{24,32},{32,40},{40,48},{48,56},{56,64},{64,7... | collective-permute-start | bytes 786440 | tf_op jit(solution)/shard_map/while/body/eval_jaxpr/ppermute | solution.py:14
  200.2 11.8 %collective-permute-start = (f32[4,128,128]{2,1,0:T(8,128)}, f32[4,128,128]{2,1,0:T(8,128)S(1)}, u32[]{:S(2)}, u32[]{:S(2)}) collective-permute-start(f32[4,128,128]{2,1,0:T(8,128)} %add.116), channel_id=1, source_target_pairs={{0,8},{8,16},{16,24},{24,32},{32,40},{40,48},{48,56},{56,64},{64,7... | collective-permute-start | bytes 786440 | tf_op jit(solution)/shard_map/while/body/eval_jaxpr/ppermute | solution.py:14
  213.7 11.8 %collective-permute-start = (f32[4,128,128]{2,1,0:T(8,128)}, f32[4,128,128]{2,1,0:T(8,128)S(1)}, u32[]{:S(2)}, u32[]{:S(2)}) collective-permute-start(f32[4,128,128]{2,1,0:T(8,128)} %add.116), channel_id=1, source_target_pairs={{0,8},{8,16},{16,24},{24,32},{32,40},{40,48},{48,56},{56,64},{64,7... | collective-permute-start | bytes 786440 | tf_op jit(solution)/shard_map/while/body/eval_jaxpr/ppermute | solution.py:14
  227.1 11.8 %collective-permute-start = (f32[4,128,128]{2,1,0:T(8,128)}, f32[4,128,128]{2,1,0:T(8,128)S(1)}, u32[]{:S(2)}, u32[]{:S(2)}) collective-permute-start(f32[4,128,128]{2,1,0:T(8,128)} %add.116), channel_id=1, source_target_pairs={{0,8},{8,16},{16,24},{24,32},{32,40},{40,48},{48,56},{56,64},{64,7... | collective-permute-start | bytes 786440 | tf_op jit(solution)/shard_map/while/body/eval_jaxpr/ppermute | solution.py:14
  240.6 11.8 %collective-permute-start = (f32[4,128,128]{2,1,0:T(8,128)}, f32[4,128,128]{2,1,0:T(8,128)S(1)}, u32[]{:S(2)}, u32[]{:S(2)}) collective-permute-start(f32[4,128,128]{2,1,0:T(8,128)} %add.116), channel_id=1, source_target_pairs={{0,8},{8,16},{16,24},{24,32},{32,40},{40,48},{48,56},{56,64},{64,7... | collective-permute-start | bytes 786440 | tf_op jit(solution)/shard_map/while/body/eval_jaxpr/ppermute | solution.py:14
  254.1 12.6 %collective-permute-start = (f32[4,128,128]{2,1,0:T(8,128)}, f32[4,128,128]{2,1,0:T(8,128)S(1)}, u32[]{:S(2)}, u32[]{:S(2)}) collective-permute-start(f32[4,128,128]{2,1,0:T(8,128)} %add.116), channel_id=1, source_target_pairs={{0,8},{8,16},{16,24},{24,32},{32,40},{40,48},{48,56},{56,64},{64,7... | collective-permute-start | bytes 786440 | tf_op jit(solution)/shard_map/while/body/eval_jaxpr/ppermute | solution.py:14
  268.4 13.8 %collective-permute-start = (f32[4,128,128]{2,1,0:T(8,128)}, f32[4,128,128]{2,1,0:T(8,128)S(1)}, u32[]{:S(2)}, u32[]{:S(2)}) collective-permute-start(f32[4,128,128]{2,1,0:T(8,128)} %add.116), channel_id=1, source_target_pairs={{0,8},{8,16},{16,24},{24,32},{32,40},{40,48},{48,56},{56,64},{64,7... | collective-permute-start | bytes 786440 | tf_op jit(solution)/shard_map/while/body/eval_jaxpr/ppermute | solution.py:14
  283.8 14.3 %collective-permute-start = (f32[4,128,128]{2,1,0:T(8,128)}, f32[4,128,128]{2,1,0:T(8,128)S(1)}, u32[]{:S(2)}, u32[]{:S(2)}) collective-permute-start(f32[4,128,128]{2,1,0:T(8,128)} %add.116), channel_id=1, source_target_pairs={{0,8},{8,16},{16,24},{24,32},{32,40},{40,48},{48,56},{56,64},{64,7... | collective-permute-start | bytes 786440 | tf_op jit(solution)/shard_map/while/body/eval_jaxpr/ppermute | solution.py:14
  299.8 13.4 %collective-permute-start = (f32[4,128,128]{2,1,0:T(8,128)}, f32[4,128,128]{2,1,0:T(8,128)S(1)}, u32[]{:S(2)}, u32[]{:S(2)}) collective-permute-start(f32[4,128,128]{2,1,0:T(8,128)} %add.116), channel_id=1, source_target_pairs={{0,8},{8,16},{16,24},{24,32},{32,40},{40,48},{48,56},{56,64},{64,7... | collective-permute-start | bytes 786440 | tf_op jit(solution)/shard_map/while/body/eval_jaxpr/ppermute | solution.py:14
  314.9 12.6 %collective-permute-start = (f32[4,128,128]{2,1,0:T(8,128)}, f32[4,128,128]{2,1,0:T(8,128)S(1)}, u32[]{:S(2)}, u32[]{:S(2)}) collective-permute-start(f32[4,128,128]{2,1,0:T(8,128)} %add.116), channel_id=1, source_target_pairs={{0,8},{8,16},{16,24},{24,32},{32,40},{40,48},{48,56},{56,64},{64,7... | collective-permute-start | bytes 786440 | tf_op jit(solution)/shard_map/while/body/eval_jaxpr/ppermute | solution.py:14
  369.5 11.8 %collective-permute-start = (f32[4,128,128]{2,1,0:T(8,128)}, f32[4,128,128]{2,1,0:T(8,128)S(1)}, u32[]{:S(2)}, u32[]{:S(2)}) collective-permute-start(f32[4,128,128]{2,1,0:T(8,128)} %add.116), channel_id=1, source_target_pairs={{0,8},{8,16},{16,24},{24,32},{32,40},{40,48},{48,56},{56,64},{64,7... | collective-permute-start | bytes 786440 | tf_op jit(solution)/shard_map/while/body/eval_jaxpr/ppermute | solution.py:14
  409.9 12.1 %collective-permute-start = (f32[4,128,128]{2,1,0:T(8,128)}, f32[4,128,128]{2,1,0:T(8,128)S(1)}, u32[]{:S(2)}, u32[]{:S(2)}) collective-permute-start(f32[4,128,128]{2,1,0:T(8,128)} %add.116), channel_id=1, source_target_pairs={{0,8},{8,16},{16,24},{24,32},{32,40},{40,48},{48,56},{56,64},{64,7... | collective-permute-start | bytes 786440 | tf_op jit(solution)/shard_map/while/body/eval_jaxpr/ppermute | solution.py:14
  423.6 13.2 %collective-permute-start = (f32[4,128,128]{2,1,0:T(8,128)}, f32[4,128,128]{2,1,0:T(8,128)S(1)}, u32[]{:S(2)}, u32[]{:S(2)}) collective-permute-start(f32[4,128,128]{2,1,0:T(8,128)} %add.116), channel_id=1, source_target_pairs={{0,8},{8,16},{16,24},{24,32},{32,40},{40,48},{48,56},{56,64},{64,7... | collective-permute-start | bytes 786440 | tf_op jit(solution)/shard_map/while/body/eval_jaxpr/ppermute | solution.py:14
  438.5 11.8 %collective-permute-start = (f32[4,128,128]{2,1,0:T(8,128)}, f32[4,128,128]{2,1,0:T(8,128)S(1)}, u32[]{:S(2)}, u32[]{:S(2)}) collective-permute-start(f32[4,128,128]{2,1,0:T(8,128)} %add.116), channel_id=1, source_target_pairs={{0,8},{8,16},{16,24},{24,32},{32,40},{40,48},{48,56},{56,64},{64,7... | collective-permute-start | bytes 786440 | tf_op jit(solution)/shard_map/while/body/eval_jaxpr/ppermute | solution.py:14
  (20 other events, 189.9 us)
